TPU v7x, 32 devices: a whole 2x2x4 slice. The times are simulated.
32 devices in a mesh: group: 2 (over y), seq: 8 (over z, x), chan: 2 (over core).
Axes of the slice: x: 2, y: 2, z: 4, core: 2. Of those that a mesh axis runs over, the one named last changes fastest.
Arguments:
- fresh: bfloat16 [2048, 3, 2048], P(('group', 'seq'), None, 'chan'), parts along dimension 0, may hold values from -6 to 6
- library: bfloat16 [8, 8, 2048], P('seq', None, 'chan'), may hold values from -6 to 6
- block_slot: int32 [8], replicated, may hold values from 0 to 7, each once
- prefix_blocks: int32 [16, 4], P('group'), parts along dimension 0, may hold values from 0 to 7, all different within a row
- short_taps: float32 [3, 3, 2048], P(None, None, 'chan'), may hold values from -4 to 4
- long_filter: float32 [1024, 2048], P('seq', 'chan'), may hold values from -2 to 2
- skip_gain: float32 [2048], P('chan'), may hold values from -6 to 6
Outputs:
- mixed: bfloat16 [2048, 2048], P(('group', 'seq'), 'chan'), parts along dimension 0
There are 2 independent parts, one for each index of `group`. A program takes and returns all parts, laid end to end along the dimension named above; an argument that names none is the same for every part. Nothing has to cross between parts.
Inputs may be any that keep to these rules, and one draw needn't show every extreme that they name: `block_slot`: each number appears once. `prefix_blocks`: every library block is named at least once; the four entries of a row differ.
All inputs are finite; a program needn't handle non-finite values.
Results may differ from a plain program's by a relative error of at most 0.008.
Values may be sent and summed in bfloat16 or wider, within the bound.
No kernel may reach another device: no remote copies, remote signals or barrier semaphores. Data moves between devices by JAX's collectives and lax.ppermute only.
A program may use at most 64 MiB of HBM per device.

v0:
```python
import math
import jax
import jax.numpy as jnp
from jax import lax
from jax.sharding import PartitionSpec as P

TAPS = 3
BLK = 8


def from_behind(shard, axis, by):
    count = lax.axis_size(axis)
    pairs = [(i, i + by) for i in range(count) if 0 <= i + by < count]
    return lax.ppermute(shard, axis, pairs)


def exact_dot(pattern, matrix, tensor):
    return jnp.einsum(pattern, matrix, tensor, precision=lax.Precision.HIGHEST)


def turn_angles(numbers, period):
    return (numbers % period).astype(jnp.float32) * (2.0 * math.pi / period)


def ring_body(fresh, library, block_slot, prefix_blocks, short_taps, long_filter, skip_gain):
    row_count = fresh.shape[0]
    channels = fresh.shape[2]
    devices = lax.axis_size("seq")
    seq_index = lax.axis_index("seq")
    group_rows = row_count // devices
    period = 2 * row_count * devices
    block_ids = jnp.arange(devices, dtype=jnp.int32)
    mode_ids = jnp.arange(2 * devices, dtype=jnp.int32)
    coarse = turn_angles(mode_ids[:, None] * block_ids[None, :], 2 * devices)
    cos_q = jnp.cos(coarse)
    sin_q = jnp.sin(coarse)
    local_rows = seq_index * group_rows + jnp.arange(group_rows, dtype=jnp.int32)
    twist = turn_angles(mode_ids[:, None] * local_rows[None, :], period)
    twist_cos = jnp.cos(twist)[:, :, None]
    twist_sin = jnp.sin(twist)[:, :, None]
    row_ids = jnp.arange(row_count, dtype=jnp.int32)
    fine_angles = turn_angles(row_ids[:, None] * row_ids[None, :], row_count)
    cos_m = jnp.cos(fine_angles)
    sin_m = jnp.sin(fine_angles)
    first_modes = 2 * seq_index + jnp.arange(2, dtype=jnp.int32)
    back_twist = turn_angles(first_modes[:, None] * row_ids[None, :], period)
    back_cos = jnp.cos(back_twist)[:, :, None]
    back_sin = jnp.sin(back_twist)[:, :, None]

    def to_modes(column):
        real_part = exact_dot("kq,qgc->kgc", cos_q, column)
        imag_part = -exact_dot("kq,qgc->kgc", sin_q, column)
        return jnp.stack(
            [
                real_part * twist_cos + imag_part * twist_sin,
                imag_part * twist_cos - real_part * twist_sin,
            ]
        )

    def to_spectrum(spread):
        real_part = exact_dot("ki,jic->jkc", cos_m, spread[0]) + exact_dot(
            "ki,jic->jkc", sin_m, spread[1]
        )
        imag_part = exact_dot("ki,jic->jkc", cos_m, spread[1]) - exact_dot(
            "ki,jic->jkc", sin_m, spread[0]
        )
        return (real_part, imag_part)

    blocks_here = row_count // BLK
    flat_ids = prefix_blocks.reshape(-1)
    first_block = jnp.minimum(seq_index * blocks_here, flat_ids.shape[0] - blocks_here)
    own_ids = lax.dynamic_slice_in_dim(flat_ids, first_block, blocks_here)
    matches = own_ids[:, None] == jnp.arange(block_slot.shape[0], dtype=jnp.int32)[None, :]
    wanted = jnp.sum(jnp.where(matches, block_slot[None, :], 0), axis=1)
    shards = lax.all_gather(library, "seq", axis=0, tiled=True)
    picker = (wanted[:, None] == jnp.arange(shards.shape[0], dtype=jnp.int32)[None, :]).astype(
        jnp.bfloat16
    )
    gathered = jnp.einsum("bn,nlc->blc", picker, shards, preferred_element_type=jnp.float32)
    cached = gathered.reshape(row_count, channels).astype(jnp.bfloat16)
    values = jnp.where(seq_index < devices // 4, cached, fresh[:, 2])
    stacked = jnp.concatenate([fresh[:, :2], values[:, None]], axis=1)
    previous = from_behind(stacked[row_count - (TAPS - 1) :], "seq", 1)
    extended = jnp.concatenate([previous, stacked], axis=0)
    shortened = jnp.zeros((row_count, 3, channels), jnp.float32)
    for offset in range(TAPS):
        window_start = TAPS - 1 - offset
        shortened = shortened + short_taps[offset][None] * extended[
            window_start : window_start + row_count
        ].astype(jnp.float32)
    gating = shortened[:, 0]
    signal = shortened[:, 1] * shortened[:, 2]
    spread_signal = to_modes(
        lax.all_to_all(signal[None], "seq", split_axis=1, concat_axis=0, tiled=True)
    )
    spread_taps = to_modes(
        lax.all_to_all(long_filter[None], "seq", split_axis=1, concat_axis=0, tiled=True)
    )
    moved_signal, moved_taps = (
        lax.all_to_all(
            spread_signal.astype(jnp.bfloat16), "seq", split_axis=1, concat_axis=2, tiled=True
        ).astype(spread_signal.dtype),
        lax.all_to_all(
            spread_taps.astype(jnp.bfloat16), "seq", split_axis=1, concat_axis=2, tiled=True
        ).astype(spread_taps.dtype),
    )
    sig_real, sig_imag = to_spectrum(moved_signal)
    tap_real, tap_imag = to_spectrum(moved_taps)
    prod_real = sig_real * tap_real - sig_imag * tap_imag
    prod_imag = sig_real * tap_imag + sig_imag * tap_real
    back_real = exact_dot("ki,jic->jkc", cos_m, prod_real) - exact_dot(
        "ki,jic->jkc", sin_m, prod_imag
    )
    back_imag = exact_dot("ki,jic->jkc", cos_m, prod_imag) + exact_dot(
        "ki,jic->jkc", sin_m, prod_real
    )
    turned = jnp.stack(
        [back_real * back_cos - back_imag * back_sin, back_imag * back_cos + back_real * back_sin]
    )
    spread = lax.all_to_all(turned, "seq", split_axis=2, concat_axis=1, tiled=True)
    positions = (
        exact_dot("kq,kgc->qgc", cos_q, spread[0]) - exact_dot("kq,kgc->qgc", sin_q, spread[1])
    ) / period
    convolved = lax.all_to_all(positions, "seq", split_axis=0, concat_axis=1, tiled=True)[0]
    output = gating * (convolved + skip_gain[None, :] * signal)
    return output.astype(jnp.bfloat16)


def dft_tables(tokens):
    period = 2 * tokens
    width = 1
    while width * width < tokens:
        width *= 2
    outer = tokens // width
    freqs = jnp.arange(tokens + 1, dtype=jnp.int32)[:, None]
    coarse = turn_angles(freqs * (width * jnp.arange(outer, dtype=jnp.int32))[None, :], period)
    fine = turn_angles(freqs * jnp.arange(width, dtype=jnp.int32)[None, :], period)
    c1, s1 = (jnp.cos(coarse)[:, :, None], jnp.sin(coarse)[:, :, None])
    c2, s2 = (jnp.cos(fine)[:, None, :], jnp.sin(fine)[:, None, :])
    cos_t = (c1 * c2 - s1 * s2).reshape(tokens + 1, tokens)
    sin_t = (s1 * c2 + c1 * s2).reshape(tokens + 1, tokens)
    return (cos_t, sin_t)


def local_body(fresh, library, block_slot, prefix_blocks, short_taps, long_filter, skip_gain):
    row_count, _, channels = fresh.shape
    devices = lax.axis_size("seq")
    seq_index = lax.axis_index("seq")
    tokens = row_count * devices
    own = channels // devices
    lib_here = library.shape[0]
    lib_rows = lib_here * BLK // 4
    packed = jnp.concatenate([fresh, long_filter.astype(jnp.bfloat16)[:, None, :]], axis=1)
    packed = jnp.concatenate([packed, library.reshape(lib_rows, 4, channels)], axis=0)
    moved = lax.all_to_all(packed, "seq", split_axis=2, concat_axis=0, tiled=True)
    moved = moved.reshape(devices, row_count + lib_rows, 4, own)
    rows = moved[:, :row_count].reshape(tokens, 4, own)
    lib_all = moved[:, row_count:].reshape(devices * lib_here, BLK * own)
    slot_ids = block_slot[prefix_blocks.reshape(-1)]
    prefix_len = slot_ids.shape[0] * BLK
    picker = (slot_ids[:, None] == jnp.arange(lib_all.shape[0], dtype=jnp.int32)[None, :]).astype(
        jnp.bfloat16
    )
    cached = jnp.dot(picker, lib_all, preferred_element_type=jnp.float32)
    cached = cached.reshape(prefix_len, own).astype(jnp.bfloat16)
    values = jnp.concatenate([cached, rows[prefix_len:, 2]], axis=0)
    stacked = jnp.concatenate([rows[:, :2], values[:, None]], axis=1).astype(jnp.float32)
    taps = lax.dynamic_slice_in_dim(short_taps, seq_index * own, own, axis=2)
    gain = lax.dynamic_slice_in_dim(skip_gain, seq_index * own, own, axis=0)
    shortened = jnp.zeros((tokens, 3, own), jnp.float32)
    for offset in range(TAPS):
        shifted = jnp.pad(stacked[: tokens - offset], ((offset, 0), (0, 0), (0, 0)))
        shortened = shortened + taps[offset][None] * shifted
    gating = shortened[:, 0]
    signal = shortened[:, 1] * shortened[:, 2]
    cos_t, sin_t = dft_tables(tokens)
    table = jnp.concatenate([cos_t, sin_t], axis=0).astype(jnp.bfloat16)
    operands = jnp.concatenate([signal.astype(jnp.bfloat16), rows[:, 3]], axis=1)
    spec = jnp.dot(table, operands, preferred_element_type=jnp.float32)
    bins = tokens + 1
    sig_c, tap_c = (spec[:bins, :own], spec[:bins, own:])
    sig_s, tap_s = (spec[bins:, :own], spec[bins:, own:])
    weight = jnp.where((jnp.arange(bins) == 0) | (jnp.arange(bins) == tokens), 1.0, 2.0).astype(
        jnp.float32
    )[:, None] / (2 * tokens)
    real = (sig_c * tap_c - sig_s * tap_s) * weight
    turned = (sig_c * tap_s + sig_s * tap_c) * weight
    back = jnp.concatenate([real, turned], axis=0).astype(jnp.bfloat16)
    convolved = lax.dot_general(
        table, back, (((0,), (0,)), ((), ())), preferred_element_type=jnp.float32
    )
    output = (gating * (convolved + gain[None, :] * signal)).astype(jnp.bfloat16)
    return lax.all_to_all(output, "seq", split_axis=0, concat_axis=1, tiled=True)


def body(fresh, library, *rest):
    devices = lax.axis_size("seq")
    tokens = fresh.shape[0] * devices
    fits = tokens <= 4096 and fresh.shape[2] % devices == 0 and (library.shape[0] * BLK % 4 == 0)
    if fits:
        return local_body(fresh, library, *rest)
    return ring_body(fresh, library, *rest)


def solution(mesh):
    return jax.shard_map(
        body,
        mesh=mesh,
        in_specs=(
            P(("group", "seq"), None, "chan"),
            P("seq", None, "chan"),
            P(),
            P("group", None),
            P(None, None, "chan"),
            P("seq", "chan"),
            P("chan"),
        ),
        out_specs=P(("group", "seq"), "chan"),
        check_vma=False,
    )
```

profile of v0, /device:TPU:0, one launch (start us, length us, event | category | flops | bytes accessed | tf_op | source)
XLA Modules:
  0.0 86.8 jit_solution(6593084510004803457)
XLA Ops:
  0.0 0.8 reshape.169
  0.8 1.1 %convert_bitcast_fusion = bf16[128,1,1024]{2,0,1:T(8,128)(2,1)S(1)} fusion(f32[128,1024]{1,0:T(8,128)} %param.12), kind=kLoop, calls=%fused_computation.27 | loop fusion | flops 131072 | bytes 786432 | tf_op jit(solution)/shard_map/broadcast_in_dim | solution.py:153
  1.9 0.4 copy.37
  2.3 0.7 copy.38
  3.1 0.7 copy.36
  3.8 2.9 %pad_maximum_fusion.3 = bf16[130,4,1024]{0,1,2:T(4,128)(2,1)} fusion(bf16[2,4,1024]{0,1,2:T(4,128)(2,1)S(1)} %copy.38, bf16[128,1,1024]{0,1,2:T(2,128)(2,1)S(1)} %copy.37, bf16[128,3,1024]{0,1,2:T(4,128)(2,1)S(1)} %copy.36), kind=kLoop, calls=%fused_computation.6 | loop fusion | flops 3194880 | bytes 2129920 | tf_op jit(solution)/shard_map/concatenate | solution.py:154
  6.7 7.4 %all-to-all-start = ((bf16[130,4,1024]{0,1,2:T(4,128)(2,1)}), bf16[130,4,1024]{0,1,2:T(4,128)(2,1)S(1)}, u32[]{:S(2)}, u32[]{:S(2)}) async-start(bf16[130,4,1024]{0,1,2:T(4,128)(2,1)} %pad_maximum_fusion.3), calls=%async_computation | async-start | bytes 4194304 | tf_op jit(solution)/shard_map/all_to_all | solution.py:155
  14.3 0.8 dynamic_slice.7
  15.0 0.7 gather_fusion
  15.7 0.7 dynamic-slice_bitcast_fusion.2
  16.5 0.6 fusion.25
  17.1 0.7 fusion.28
  17.7 3.7 %subtract_convert_fusion = (bf16[1025,32,32]{0,2,1:T(8,128)(2,1)}, bf16[1025,32,32]{0,2,1:T(8,128)(2,1)}) fusion(f32[1025,32]{0,1:T(8,128)S(1)} %get-tuple-element.14, f32[1025,32]{0,1:T(8,128)S(1)} %get-tuple-element.13, f32[1025,32]{0,1:T(8,128)S(1)} %get-tuple-element.15, f32[1025,32]{0,1:T(8,128)S(1)} %get-tuple-element.12), kind=kLoop, calls=%fused_computation.2 | loop fusion | flops 8396800 | bytes 4723200 | tf_op jit(solution)/shard_map/convert.5
  21.4 40.9 %all-to-all-done = bf16[130,4,1024]{0,1,2:T(4,128)(2,1)S(1)} async-done(((bf16[130,4,1024]{0,1,2:T(4,128)(2,1)}), bf16[130,4,1024]{0,1,2:T(4,128)(2,1)S(1)}, u32[]{:S(2)}, u32[]{:S(2)}) %all-to-all-start) | async-done | bytes 1064992 | tf_op jit(solution)/shard_map/all_to_all | solution.py:155
  62.3 3.9 %copy.43 = bf16[130,4,8,128]{3,2,1,0:T(8,128)(2,1)S(1)} copy(bf16[130,4,8,128]{0,1,3,2:T(4,128)(2,1)S(1)} %bitcast.44) | data formatting | bytes 2129920 | tf_op jit(solution)/shard_map/all_to_all | solution.py:155
  66.3 0.4 copy.40
  67.2 0.5 multiply_add_fusion
  67.9 1.0 %copy-done.1 = bf16[1025,32,32]{0,2,1:T(8,128)(2,1)S(1)} copy-done((bf16[1025,32,32]{0,2,1:T(8,128)(2,1)S(1)}, bf16[1025,32,32]{0,2,1:T(8,128)(2,1)}, u32[]{:S(2)}) %copy-start.1) | copy-done | bytes 2099224
  68.9 0.7 copy-done.2
  69.6 2.2 %fusion.1 = f32[2050,256]{1,0:T(8,128)S(1)} fusion(bf16[1025,1024]{0,1:T(8,128)(2,1)S(1)} %bitcast.52, bf16[1025,1024]{0,1:T(8,128)(2,1)S(1)} %bitcast.50, bf16[1024,128]{1,0:T(8,128)(2,1)S(1)} %slice_bitcast_fusion.1, bf16[1024,128]{1,0:T(8,128)(2,1)S(1)} %fusion.12), kind=kOutput, calls=%fused_computation.5 | convolution fusion | flops 1084235776 | bytes 6821888 | tf_op jit(solution)/shard_map/dot_general | solution.py:179
  71.8 0.3 multiply_convert_fusion.1
  72.1 1.4 %fusion.4 = bf16[1024,128]{1,0:T(8,128)(2,1)S(1)} fusion(bf16[1025,1024]{0,1:T(8,128)(2,1)S(1)} %bitcast.53, bf16[1025,1024]{0,1:T(8,128)(2,1)S(1)} %bitcast.51, bf16[1025,128]{1,0:T(8,128)(2,1)S(1)} %get-tuple-element.6, bf16[1025,128]{1,0:T(8,128)(2,1)S(1)} %get-tuple-element.5, f32[1024,3,128]{2,0,1:T(8,128)S(1)} %multiply_add_fusion, ...), kind=kOutput, calls=%fused_computation.10 | convolution fusion | flops 547496960 | bytes 6558720 | tf_op jit(solution)/shard_map/dot_general | solution.py:189
  73.5 12.5 %all_to_all.34 = bf16[8,128,128]{2,1,0:T(8,128)(2,1)S(1)} all-to-all(bf16[8,128,128]{2,1,0:T(8,128)(2,1)S(1)} %bitcast.54), channel_id=1, replica_groups=mesh['group'=2,'seq'=8,'chan'=2] {'seq'}, dimensions={0} | all-to-all | bytes 524288 | tf_op jit(solution)/shard_map/all_to_all | solution.py:193
  86.0 0.7 copy_bitcast_fusion
  (24 shorter events, 0.8 us)
Async XLA Ops:
  0.0 15.0 %copy-start = (s32[8]{0:T(128)S(1)}, s32[8]{0:T(128)}, u32[]{:S(2)}) copy-start(s32[8]{0:T(128)} %param.9) | copy-start | bytes 100
  0.0 3.1 %copy-start.3 = (bf16[128,3,1024]{2,0,1:T(8,128)(2,1)S(1)}, bf16[128,3,1024]{2,0,1:T(8,128)(2,1)}, u32[]{:S(2)}) copy-start(bf16[128,3,1024]{2,0,1:T(8,128)(2,1)} %param.7) | copy-start | bytes 2359300
  6.7 7.4 %copy-start.4 = (s32[8,4]{0,1:T(4,128)S(1)}, s32[8,4]{0,1:T(4,128)}, u32[]{:S(2)}) copy-start(s32[8,4]{0,1:T(4,128)} %param.10) | copy-start | bytes 388
  6.7 55.7 %all-to-all-start = ((bf16[130,4,1024]{0,1,2:T(4,128)(2,1)}), bf16[130,4,1024]{0,1,2:T(4,128)(2,1)S(1)}, u32[]{:S(2)}, u32[]{:S(2)}) async-start(bf16[130,4,1024]{0,1,2:T(4,128)(2,1)} %pad_maximum_fusion.3), calls=%async_computation | async-start | bytes 4194304 | tf_op jit(solution)/shard_map/all_to_all | solution.py:155
  67.2 1.7 %copy-start.1 = (bf16[1025,32,32]{0,2,1:T(8,128)(2,1)S(1)}, bf16[1025,32,32]{0,2,1:T(8,128)(2,1)}, u32[]{:S(2)}) copy-start(bf16[1025,32,32]{0,2,1:T(8,128)(2,1)} %get-tuple-element.7) | copy-start | bytes 6297604
  67.2 2.4 %copy-start.2 = (bf16[1025,32,32]{0,2,1:T(8,128)(2,1)S(1)}, bf16[1025,32,32]{0,2,1:T(8,128)(2,1)}, u32[]{:S(2)}) copy-start(bf16[1025,32,32]{0,2,1:T(8,128)(2,1)} %get-tuple-element.8) | copy-start | bytes 6297604
where the time goes:
time: 87.2 us; the launch traced here: 86.8 us
  waiting for transfers between devices  40.9 us (47%)
  blocking collectives  12.5 us (14%)
  local copies, waits for them, and re-layouts  12 us (14%)
  other arithmetic  9.91 us (11%)
  starting transfers between devices  7.41 us (8%)
  matrix products  3.8 us (4%)
    all_to_all x1, waiting for transfers between devices, local_body(): lax.all_to_all(packed, 'seq', split_axis=2, concat_axis=0, tiled=True)  40.9 us
    all_to_all x1, blocking collectives, local_body(): lax.all_to_all(output, 'seq', split_axis=0, concat_axis=1, tiled=True)  12.5 us
    all_to_all x1, starting transfers between devices, local_body(): lax.all_to_all(packed, 'seq', split_axis=2, concat_axis=0, tiled=True)  7.41 us
    another operation x2, other arithmetic  3.99 us
    all_to_all x1, local copies, waits for them, and re-layouts, local_body(): lax.all_to_all(packed, 'seq', split_axis=2, concat_axis=0, tiled=True)  3.92 us
    concatenate x1, other arithmetic, local_body(): jnp.concatenate([packed, library.reshape(lib_rows, 4, channels)], axis=0)  2.86 us
    unnamed x12, local copies, waits for them, and re-layouts  2.58 us
    dot_general x1, matrix products, local_body(): spec = jnp.dot(table, operands, preferred_element_type=jnp.float32)  2.2 us
  transfers between devices with their start and end apart: 1, of which 1 were waited for; matrix products, arithmetic and copies ran while one was open for 8% of the time, Pallas kernels for 0%

commit v1 on v0

--- a/solution.py
+++ b/solution.py
@@ -152,7 +152,19 @@
     lib_rows = lib_here * BLK // 4
     packed = jnp.concatenate([fresh, long_filter.astype(jnp.bfloat16)[:, None, :]], axis=1)
     packed = jnp.concatenate([packed, library.reshape(lib_rows, 4, channels)], axis=0)
-    moved = lax.all_to_all(packed, "seq", split_axis=2, concat_axis=0, tiled=True)
+    ways, here = (lax.axis_size("seq"), lax.axis_index("seq"))
+    width_2 = packed.shape[2] // ways
+    shape = list(packed.shape)
+    shape[2] = width_2
+    height = shape[0]
+    shape[0] = height * ways
+    full = jnp.zeros(shape, packed.dtype)
+    for mask in range(ways):
+        part = lax.dynamic_slice_in_dim(packed, (here ^ mask) * width_2, width_2, axis=2)
+        if mask:
+            part = lax.ppermute(part, "seq", [(d, d ^ mask) for d in range(ways)])
+        full = lax.dynamic_update_slice_in_dim(full, part, (here ^ mask) * height, axis=0)
+    moved = full
     moved = moved.reshape(devices, row_count + lib_rows, 4, own)
     rows = moved[:, :row_count].reshape(tokens, 4, own)
     lib_all = moved[:, row_count:].reshape(devices * lib_here, BLK * own)

time: 87.2 us -> 57.5 us (0.66)
  waiting for transfers between devices: 40.9 us -> 5.67 us
  starting transfers between devices: 7.41 us -> 14.6 us
  other arithmetic: 9.91 us -> 8.22 us
  blocking collectives: 12.5 us -> 13.9 us
  local copies, waits for them, and re-layouts: 12 us -> 10.7 us
    all_to_all x1 -> x0, waiting for transfers between devices: 40.9 us -> none  [local_body(): lax.all_to_all(packed, 'seq', split_axis=2, concat_axis=0, tiled=True)]
    ppermute x0 -> x7, starting transfers between devices: none -> 14.6 us  [local_body(): part = lax.ppermute(part, 'seq', [(d, d ^ mask) for d in range(ways)])]
    all_to_all x1 -> x0, starting transfers between devices: 7.41 us -> none  [local_body(): lax.all_to_all(packed, 'seq', split_axis=2, concat_axis=0, tiled=True)]
    ppermute x0 -> x7, waiting for transfers between devices: none -> 5.67 us  [local_body(): part = lax.ppermute(part, 'seq', [(d, d ^ mask) for d in range(ways)])]
    dynamic_update_slice x0 -> x8, local copies, waits for them, and re-layouts: none -> 4.02 us  [local_body(): lax.dynamic_update_slice_in_dim(full, part, (here ^ mask) * height, axis=0)]
    all_to_all x1 -> x0, local copies, waits for them, and re-layouts: 3.92 us -> none  [local_body(): lax.all_to_all(packed, 'seq', split_axis=2, concat_axis=0, tiled=True)]
    concatenate x1, other arithmetic: 2.86 us -> 1.24 us  [local_body(): jnp.concatenate([packed, library.reshape(lib_rows, 4, channels)], axis=0)]
    all_to_all x1, blocking collectives: 12.5 us -> 13.9 us  [local_body(): lax.all_to_all(output, 'seq', split_axis=0, concat_axis=1, tiled=True)]
  transfers between devices with their start and end apart: 1 -> 7, of which waited for: 1 -> 3; matrix products, arithmetic and copies ran while one was open for 8% -> 19% of each run, Pallas kernels for 0% -> 0%
where the time goes in v1:
time: 57.5 us; the launch traced here: 57.2 us
  starting transfers between devices  14.6 us (25%)
  blocking collectives  13.9 us (24%)
  local copies, waits for them, and re-layouts  10.7 us (19%)
  other arithmetic  8.22 us (14%)
  waiting for transfers between devices  5.67 us (10%)
  matrix products  3.79 us (7%)
    ppermute x7, starting transfers between devices, local_body(): part = lax.ppermute(part, 'seq', [(d, d ^ mask) for d in range(ways)])  14.6 us
    all_to_all x1, blocking collectives, local_body(): lax.all_to_all(output, 'seq', split_axis=0, concat_axis=1, tiled=True)  13.9 us
    ppermute x7, waiting for transfers between devices, local_body(): part = lax.ppermute(part, 'seq', [(d, d ^ mask) for d in range(ways)])  5.67 us
    dynamic_update_slice x8, local copies, waits for them, and re-layouts, local_body(): lax.dynamic_update_slice_in_dim(full, part, (here ^ mask) * height, axis=0)  4.02 us
    another operation x2, other arithmetic  3.93 us
    dot_general x1, matrix products, local_body(): spec = jnp.dot(table, operands, preferred_element_type=jnp.float32)  2.19 us
    unnamed x9, local copies, waits for them, and re-layouts  1.85 us
    dot_general x1, matrix products, local_body(): lax.dot_general(table, back, (((0,), (0,)), ((), ())), preferred_element_...  1.39 us
  transfers between devices with their start and end apart: 7, of which 3 were waited for; matrix products, arithmetic and copies ran while one was open for 19% of the time, Pallas kernels for 0%

profile of v1, /device:TPU:0, one launch (start us, length us, event | category | flops | bytes accessed | tf_op | source)
XLA Modules:
  0.0 57.2 jit_solution(17596991148796696554)
XLA Ops:
  0.0 0.7 %reshape.170 = bf16[2,4,1024]{2,1,0:T(4,128)(2,1)S(1)} reshape(bf16[1,8,1024]{2,1,0:T(8,128)(2,1)} %param.8) | data formatting | bytes 32768 | tf_op jit(solution)/shard_map/reshape | solution.py:154
  0.8 1.1 %convert_bitcast_fusion = bf16[128,1,1024]{2,0,1:T(8,128)(2,1)S(1)} fusion(f32[128,1024]{1,0:T(8,128)} %param.12), kind=kLoop, calls=%fused_computation.27 | loop fusion | flops 131072 | bytes 786432 | tf_op jit(solution)/shard_map/broadcast_in_dim | solution.py:153
  1.9 1.2 %pad_maximum_fusion.9 = bf16[130,4,1024]{2,0,1:T(8,128)(2,1)S(1)} fusion(bf16[2,4,1024]{2,0,1:T(2,128)(2,1)S(1)} %copy.11, bf16[128,1,1024]{2,0,1:T(8,128)(2,1)S(1)} %convert_bitcast_fusion, bf16[128,3,1024]{2,0,1:T(8,128)(2,1)} %param.7), kind=kLoop, calls=%fused_computation.11 | loop fusion | flops 3194880 | bytes 2129920 | tf_op jit(solution)/shard_map/concatenate | solution.py:154
  3.5 6.1 %collective-permute-start.6 = (bf16[130,4,128]{2,0,1:T(8,128)(2,1)S(1)}, bf16[130,4,128]{2,0,1:T(8,128)(2,1)S(1)}, u32[]{:S(2)}, u32[]{:S(2)}) collective-permute-start(bf16[130,4,128]{2,0,1:T(8,128)(2,1)S(1)} %get-tuple-element.7), channel_id=1, source_target_pairs={{0,14},{2,12},{4,10},{6,8},{8,6},{10,4},{12,2},{14,0},{1,15},{3,13... | collective-permute-start | bytes 399368 | tf_op jit(solution)/shard_map/ppermute | solution.py:165
  9.8 0.8 %collective-permute-start.4 = (bf16[130,4,128]{2,0,1:T(8,128)(2,1)S(1)}, bf16[130,4,128]{2,0,1:T(8,128)(2,1)S(1)}, u32[]{:S(2)}, u32[]{:S(2)}) collective-permute-start(bf16[130,4,128]{2,0,1:T(8,128)(2,1)S(1)} %get-tuple-element.9), channel_id=1, source_target_pairs={{0,10},{2,8},{4,14},{6,12},{8,2},{10,0},{12,6},{14,4},{1,11},{3,9}... | collective-permute-start | bytes 399368 | tf_op jit(solution)/shard_map/ppermute | solution.py:165
  10.5 3.4 %collective-permute-start.1 = (bf16[130,4,128]{2,0,1:T(8,128)(2,1)S(1)}, bf16[130,4,128]{2,0,1:T(8,128)(2,1)S(1)}, u32[]{:S(2)}, u32[]{:S(2)}) collective-permute-start(bf16[130,4,128]{2,0,1:T(8,128)(2,1)S(1)} %get-tuple-element.12), channel_id=1, source_target_pairs={{0,4},{2,6},{4,0},{6,2},{8,12},{10,14},{12,8},{14,10},{1,5},{3,7},... | collective-permute-start | bytes 399368 | tf_op jit(solution)/shard_map/ppermute | solution.py:165
  13.9 1.5 %collective-permute-start = (bf16[130,4,128]{2,0,1:T(8,128)(2,1)S(1)}, bf16[130,4,128]{2,0,1:T(8,128)(2,1)S(1)}, u32[]{:S(2)}, u32[]{:S(2)}) collective-permute-start(bf16[130,4,128]{2,0,1:T(8,128)(2,1)S(1)} %get-tuple-element.13), channel_id=1, source_target_pairs={{0,2},{2,0},{4,6},{6,4},{8,10},{10,8},{12,14},{14,12},{1,3},{3,1},... | collective-permute-start | bytes 399368 | tf_op jit(solution)/shard_map/ppermute | solution.py:165
  15.4 0.6 %fusion.25 = (f32[1025,32]{0,1:T(8,128)S(1)}, f32[1025,32]{0,1:T(8,128)S(1)}) fusion(), kind=kLoop, calls=%fused_computation.48 | loop fusion | flops 459200 | bytes 262400 | tf_op jit(solution)/shard_map/sin | solution.py:139
  16.2 0.7 %fusion.28 = (f32[1025,32]{0,1:T(8,128)S(1)}, f32[1025,32]{0,1:T(8,128)S(1)}) fusion(s32[32]{0:T(128)S(1)} %iota_multiply_fusion), kind=kLoop, calls=%fused_computation.51 | loop fusion | flops 459200 | bytes 262528 | tf_op jit(solution)/shard_map/cos | solution.py:138
  16.8 3.7 %subtract_convert_fusion = (bf16[1025,32,32]{0,2,1:T(8,128)(2,1)}, bf16[1025,32,32]{0,2,1:T(8,128)(2,1)}) fusion(f32[1025,32]{0,1:T(8,128)S(1)} %get-tuple-element.22, f32[1025,32]{0,1:T(8,128)S(1)} %get-tuple-element.21, f32[1025,32]{0,1:T(8,128)S(1)} %get-tuple-element.23, f32[1025,32]{0,1:T(8,128)S(1)} %get-tuple-element.20), kind=kLoop, calls=%fused_computation.2 | loop fusion | flops 8396800 | bytes 4723200 | tf_op jit(solution)/shard_map/convert.5
  20.5 0.7 %fusion.32 = (f32[3,128]{1,0:T(4,128)S(1)}, f32[3,128]{1,0:T(4,128)S(1)}, f32[3,128]{1,0:T(4,128)S(1)}) fusion(f32[3,3,1024]{2,1,0:T(4,128)} %param.11, s32[]{:T(128)S(6)} %select_n.99, s32[]{:T(128)S(6)} %add.140, s32[]{:T(128)S(6)} %add.141), kind=kLoop, calls=%fused_computation.72 | loop fusion | bytes 9228 | tf_op jit(solution)/shard_map/mul | solution.py:185
  21.5 1.5 %collective-permute-start.3 = (bf16[130,4,128]{2,0,1:T(8,128)(2,1)S(1)}, bf16[130,4,128]{2,0,1:T(8,128)(2,1)S(1)}, u32[]{:S(2)}, u32[]{:S(2)}) collective-permute-start(bf16[130,4,128]{2,0,1:T(8,128)(2,1)S(1)} %get-tuple-element.10), channel_id=1, source_target_pairs={{0,8},{2,10},{4,12},{6,14},{8,0},{10,2},{12,4},{14,6},{1,9},{3,11}... | collective-permute-start | bytes 399368 | tf_op jit(solution)/shard_map/ppermute | solution.py:165
  23.0 1.2 %collective-permute-start.2 = (bf16[130,4,128]{2,0,1:T(8,128)(2,1)S(1)}, bf16[130,4,128]{2,0,1:T(8,128)(2,1)S(1)}, u32[]{:S(2)}, u32[]{:S(2)}) collective-permute-start(bf16[130,4,128]{2,0,1:T(8,128)(2,1)S(1)} %get-tuple-element.11), channel_id=1, source_target_pairs={{0,6},{2,4},{4,2},{6,0},{8,14},{10,12},{12,10},{14,8},{1,7},{3,5},... | collective-permute-start | bytes 399368 | tf_op jit(solution)/shard_map/ppermute | solution.py:165
  24.3 0.8 %dynamic_slice.39 = f32[128]{0:T(128)S(1)} dynamic-slice(f32[1024]{0:T(1024)} %param.13, s32[]{:T(128)S(6)} %select_n.99), dynamic_slice_sizes={128} | dynamic-slice | bytes 1028 | tf_op jit(solution)/shard_map/dynamic_slice | solution.py:181
  25.0 0.7 %gather_fusion = s32[32]{0:T(128)S(1)} fusion(s32[8]{0:T(128)S(1)} %copy-done, s32[1024]{0:T(1024)S(1)} %pad_clamp_fusion), kind=kCustom, calls=%fused_computation | custom fusion | bytes 384 | tf_op jit(solution)/shard_map/gather | solution.py:171
  27.5 2.9 %collective-permute-done.2 = bf16[130,4,128]{2,0,1:T(8,128)(2,1)S(1)} collective-permute-done((bf16[130,4,128]{2,0,1:T(8,128)(2,1)S(1)}, bf16[130,4,128]{2,0,1:T(8,128)(2,1)S(1)}, u32[]{:S(2)}, u32[]{:S(2)}) %collective-permute-start.2) | collective-permute-done | bytes 133152 | tf_op jit(solution)/shard_map/ppermute | solution.py:165
  30.9 2.4 %collective-permute-done.3 = bf16[130,4,128]{2,0,1:T(8,128)(2,1)S(1)} collective-permute-done((bf16[130,4,128]{2,0,1:T(8,128)(2,1)S(1)}, bf16[130,4,128]{2,0,1:T(8,128)(2,1)S(1)}, u32[]{:S(2)}, u32[]{:S(2)}) %collective-permute-start.3) | collective-permute-done | bytes 133152 | tf_op jit(solution)/shard_map/ppermute | solution.py:165
  36.3 0.5 multiply_add_fusion
  36.9 1.0 %copy-done.1 = bf16[1025,32,32]{0,2,1:T(8,128)(2,1)S(1)} copy-done((bf16[1025,32,32]{0,2,1:T(8,128)(2,1)S(1)}, bf16[1025,32,32]{0,2,1:T(8,128)(2,1)}, u32[]{:S(2)}) %copy-start.1) | copy-done | bytes 2099224
  38.0 0.7 %copy-done.2 = bf16[1025,32,32]{0,2,1:T(8,128)(2,1)S(1)} copy-done((bf16[1025,32,32]{0,2,1:T(8,128)(2,1)S(1)}, bf16[1025,32,32]{0,2,1:T(8,128)(2,1)}, u32[]{:S(2)}) %copy-start.2) | copy-done | bytes 2099224
  38.7 2.2 %fusion.1 = f32[2050,256]{1,0:T(8,128)S(1)} fusion(bf16[1025,1024]{0,1:T(8,128)(2,1)S(1)} %bitcast.49, bf16[1025,1024]{0,1:T(8,128)(2,1)S(1)} %bitcast.47, bf16[1024,128]{1,0:T(8,128)(2,1)S(1)} %slice_bitcast_fusion.1, bf16[1024,128]{1,0:T(8,128)(2,1)S(1)} %fusion.12), kind=kOutput, calls=%fused_computation.5 | convolution fusion | flops 1084235776 | bytes 6821888 | tf_op jit(solution)/shard_map/dot_general | solution.py:191
  41.2 1.4 %fusion.4 = bf16[1024,128]{1,0:T(8,128)(2,1)S(1)} fusion(bf16[1025,1024]{0,1:T(8,128)(2,1)S(1)} %bitcast.50, bf16[1025,1024]{0,1:T(8,128)(2,1)S(1)} %bitcast.48, bf16[1025,128]{1,0:T(8,128)(2,1)S(1)} %get-tuple-element.6, bf16[1025,128]{1,0:T(8,128)(2,1)S(1)} %get-tuple-element.5, f32[1024,3,128]{2,0,1:T(8,128)S(1)} %multiply_add_fusion, ...), kind=kOutput, calls=%fused_computation.9 | convolution fusion | flops 547496960 | bytes 6558720 | tf_op jit(solution)/shard_map/dot_general | solution.py:201
  42.6 13.9 %all_to_all.19 = bf16[8,128,128]{2,1,0:T(8,128)(2,1)S(1)} all-to-all(bf16[8,128,128]{2,1,0:T(8,128)(2,1)S(1)} %bitcast.51), channel_id=1, replica_groups=mesh['group'=2,'seq'=8,'chan'=2] {'seq'}, dimensions={0} | all-to-all | bytes 524288 | tf_op jit(solution)/shard_map/all_to_all | solution.py:205
  56.4 0.7 %copy_bitcast_fusion = bf16[128,1024]{1,0:T(8,128)(2,1)} fusion(bf16[8,128,128]{2,1,0:T(8,128)(2,1)S(1)} %all_to_all.19), kind=kLoop, calls=%fused_computation.24 | loop fusion | bytes 524288 | tf_op jit(solution)/shard_map/all_to_all | solution.py:205
  (42 shorter events, 6.5 us)
Async XLA Ops:
  0.0 25.0 %copy-start = (s32[8]{0:T(128)S(1)}, s32[8]{0:T(128)}, u32[]{:S(2)}) copy-start(s32[8]{0:T(128)} %param.9) | copy-start | bytes 100
  1.9 14.1 %copy-start.3 = (s32[8,4]{0,1:T(4,128)S(1)}, s32[8,4]{0,1:T(4,128)}, u32[]{:S(2)}) copy-start(s32[8,4]{0,1:T(4,128)} %param.10) | copy-start | bytes 388
  3.5 31.4 %collective-permute-start.6 = (bf16[130,4,128]{2,0,1:T(8,128)(2,1)S(1)}, bf16[130,4,128]{2,0,1:T(8,128)(2,1)S(1)}, u32[]{:S(2)}, u32[]{:S(2)}) collective-permute-start(bf16[130,4,128]{2,0,1:T(8,128)(2,1)S(1)} %get-tuple-element.7), channel_id=1, source_target_pairs={{0,14},{2,12},{4,10},{6,8},{8,6},{10,4},{12,2},{14,0},{1,15},{3,13... | collective-permute-start | bytes 399368 | tf_op jit(solution)/shard_map/ppermute | solution.py:165
  9.5 24.8 %collective-permute-start.5 = (bf16[130,4,128]{2,0,1:T(8,128)(2,1)S(1)}, bf16[130,4,128]{2,0,1:T(8,128)(2,1)S(1)}, u32[]{:S(2)}, u32[]{:S(2)}) collective-permute-start(bf16[130,4,128]{2,0,1:T(8,128)(2,1)S(1)} %get-tuple-element.8), channel_id=1, source_target_pairs={{0,12},{2,14},{4,8},{6,10},{8,4},{10,6},{12,0},{14,2},{1,13},{3,15... | collective-permute-start | bytes 399368 | tf_op jit(solution)/shard_map/ppermute | solution.py:165
  9.8 24.0 %collective-permute-start.4 = (bf16[130,4,128]{2,0,1:T(8,128)(2,1)S(1)}, bf16[130,4,128]{2,0,1:T(8,128)(2,1)S(1)}, u32[]{:S(2)}, u32[]{:S(2)}) collective-permute-start(bf16[130,4,128]{2,0,1:T(8,128)(2,1)S(1)} %get-tuple-element.9), channel_id=1, source_target_pairs={{0,10},{2,8},{4,14},{6,12},{8,2},{10,0},{12,6},{14,4},{1,11},{3,9}... | collective-permute-start | bytes 399368 | tf_op jit(solution)/shard_map/ppermute | solution.py:165
  10.5 11.0 %collective-permute-start.1 = (bf16[130,4,128]{2,0,1:T(8,128)(2,1)S(1)}, bf16[130,4,128]{2,0,1:T(8,128)(2,1)S(1)}, u32[]{:S(2)}, u32[]{:S(2)}) collective-permute-start(bf16[130,4,128]{2,0,1:T(8,128)(2,1)S(1)} %get-tuple-element.12), channel_id=1, source_target_pairs={{0,4},{2,6},{4,0},{6,2},{8,12},{10,14},{12,8},{14,10},{1,5},{3,7},... | collective-permute-start | bytes 399368 | tf_op jit(solution)/shard_map/ppermute | solution.py:165
  13.9 9.1 %collective-permute-start = (bf16[130,4,128]{2,0,1:T(8,128)(2,1)S(1)}, bf16[130,4,128]{2,0,1:T(8,128)(2,1)S(1)}, u32[]{:S(2)}, u32[]{:S(2)}) collective-permute-start(bf16[130,4,128]{2,0,1:T(8,128)(2,1)S(1)} %get-tuple-element.13), channel_id=1, source_target_pairs={{0,2},{2,0},{4,6},{6,4},{8,10},{10,8},{12,14},{14,12},{1,3},{3,1},... | collective-permute-start | bytes 399368 | tf_op jit(solution)/shard_map/ppermute | solution.py:165
  21.5 11.8 %collective-permute-start.3 = (bf16[130,4,128]{2,0,1:T(8,128)(2,1)S(1)}, bf16[130,4,128]{2,0,1:T(8,128)(2,1)S(1)}, u32[]{:S(2)}, u32[]{:S(2)}) collective-permute-start(bf16[130,4,128]{2,0,1:T(8,128)(2,1)S(1)} %get-tuple-element.10), channel_id=1, source_target_pairs={{0,8},{2,10},{4,12},{6,14},{8,0},{10,2},{12,4},{14,6},{1,9},{3,11}... | collective-permute-start | bytes 399368 | tf_op jit(solution)/shard_map/ppermute | solution.py:165
  23.0 7.4 %collective-permute-start.2 = (bf16[130,4,128]{2,0,1:T(8,128)(2,1)S(1)}, bf16[130,4,128]{2,0,1:T(8,128)(2,1)S(1)}, u32[]{:S(2)}, u32[]{:S(2)}) collective-permute-start(bf16[130,4,128]{2,0,1:T(8,128)(2,1)S(1)} %get-tuple-element.11), channel_id=1, source_target_pairs={{0,6},{2,4},{4,2},{6,0},{8,14},{10,12},{12,10},{14,8},{1,7},{3,5},... | collective-permute-start | bytes 399368 | tf_op jit(solution)/shard_map/ppermute | solution.py:165
  36.3 1.7 %copy-start.1 = (bf16[1025,32,32]{0,2,1:T(8,128)(2,1)S(1)}, bf16[1025,32,32]{0,2,1:T(8,128)(2,1)}, u32[]{:S(2)}) copy-start(bf16[1025,32,32]{0,2,1:T(8,128)(2,1)} %get-tuple-element.15) | copy-start | bytes 6297604
  36.3 2.4 %copy-start.2 = (bf16[1025,32,32]{0,2,1:T(8,128)(2,1)S(1)}, bf16[1025,32,32]{0,2,1:T(8,128)(2,1)}, u32[]{:S(2)}) copy-start(bf16[1025,32,32]{0,2,1:T(8,128)(2,1)} %get-tuple-element.16) | copy-start | bytes 6297604
